TPU v7x, 512 devices: a whole 4x8x8 slice. The times are simulated.
512 devices in a mesh: req: 128 (over y, z, core), tp: 4 (over x).
Axes of the slice: x: 4, y: 8, z: 8, core: 2. Of those that a mesh axis runs over, the one named last changes fastest.
Arguments:
- tokens: bfloat16 [65536, 1024], P('req', 'tp')
- placement: int32 [16384], P('req'), may hold values from 0 to 16383, as said below
- cache_len: int32 [256], P('req'), may hold values from 0 to 1024, as said below
- w_query: bfloat16 [1024, 1024], P(None, 'tp'), may hold values from -0.1875 to 0.1875
- w_key: bfloat16 [1024, 1024], P(None, 'tp'), may hold values from -0.1875 to 0.1875
- w_value: bfloat16 [1024, 1024], P(None, 'tp'), may hold values from -0.1875 to 0.1875
- w_out: bfloat16 [1024, 1024], P('tp'), may hold values from -0.1875 to 0.1875
- k_cache: bfloat16 [256, 1024, 1024], P('req', None, 'tp'), may hold values from -6 to 6
- v_cache: bfloat16 [256, 1024, 1024], P('req', None, 'tp'), may hold values from -6 to 6
- ln_gain: float32 [1024], replicated, may hold values from 0.1 to 1.9
- ln_bias: float32 [1024], replicated, may hold values from -0.5 to 0.5
Outputs:
- mixed: bfloat16 [65536, 1024], P('req', 'tp')
Inputs may be any that keep to these rules, and one draw needn't show every extreme that they name: `placement`: A permutation of the blocks. Of the 128 blocks that arrive on index s of req, exactly one goes to the owner range of every index t of req, and it lands at owner position t * 128 + s. `cache_len`: some request has exactly 1024 cached positions.
All inputs are finite; a program needn't handle non-finite values.
Results may differ from a plain program's by a relative error of at most 0.014.
The roundings to bfloat16 on the way count: a program that leaves them out, or rounds other values in their place, can miss the bound.
Values may be sent and summed in bfloat16 or wider, within the bound.
No kernel may reach another device: no remote copies, remote signals or barrier semaphores. Data moves between devices by JAX's collectives and lax.ppermute only.
A program may use at most 64 MiB of HBM per device.

v0:
```python
import jax
import jax.numpy as jnp
from jax import lax
from jax.sharding import PartitionSpec as P

D = 1024
HEADS = 16


def head_view(array, head_size):
    return array.reshape(array.shape[0], array.shape[1] // head_size, head_size)


def attend_padded(queries, new_keys, new_values, cache_keys, cache_values, length):
    head_size = D // HEADS
    new_count = queries.shape[0]
    span = cache_keys.shape[0]
    keys_all = head_view(jnp.concatenate([cache_keys, new_keys], 0), head_size)
    values_all = head_view(jnp.concatenate([cache_values, new_values], 0), head_size)
    query_heads = head_view(queries, head_size)
    scores = jnp.einsum(
        "qhd,khd->hqk", query_heads, keys_all, preferred_element_type=jnp.float32
    ) * head_size ** (-0.5)
    key_pos = jnp.arange(span + new_count, dtype=jnp.int32)[None, :]
    query_pos = jnp.arange(new_count, dtype=jnp.int32)[:, None]
    valid = jnp.where(key_pos < span, key_pos < length, key_pos - span <= query_pos)
    scores = jnp.where(valid[None], scores, -jnp.inf)
    top = jnp.max(scores, axis=-1, keepdims=True)
    weight = jnp.where(valid[None], jnp.exp(scores - top), 0.0)
    total = jnp.sum(weight, axis=-1)
    context = jnp.einsum(
        "hqk,khd->qhd", weight.astype(jnp.bfloat16), values_all, preferred_element_type=jnp.float32
    )
    context = context / jnp.transpose(total)[:, :, None]
    return context.reshape(new_count, queries.shape[1]).astype(jnp.bfloat16)


def attend_all(queries, new_keys, new_values, k_cache, v_cache, cache_len):
    request_count = k_cache.shape[0]
    req_shape = (request_count, queries.shape[0] // request_count, queries.shape[1])
    context = lax.map(
        lambda items: attend_padded(*items),
        (
            queries.reshape(req_shape),
            new_keys.reshape(req_shape),
            new_values.reshape(req_shape),
            k_cache,
            v_cache,
            cache_len,
        ),
    )
    return context.reshape(queries.shape)


def project_rows(whole, w_query, w_key, w_value):
    queries = jnp.dot(whole, w_query, preferred_element_type=jnp.float32).astype(jnp.bfloat16)
    new_keys = jnp.dot(whole, w_key, preferred_element_type=jnp.float32).astype(jnp.bfloat16)
    new_values = jnp.dot(whole, w_value, preferred_element_type=jnp.float32).astype(jnp.bfloat16)
    return (queries, new_keys, new_values)


def finish_rows(context, local, w_out, ln_gain, ln_bias):
    row_count, feat_width = local.shape
    partial_sum = jnp.dot(context, w_out, preferred_element_type=jnp.float32)
    attended = lax.psum_scatter(
        partial_sum.astype(jnp.bfloat16), "tp", scatter_dimension=1, tiled=True
    ).astype(jnp.float32)
    summed = local.astype(jnp.float32) + attended
    first_sum, square_sum = lax.psum(
        (jnp.sum(summed, axis=1), jnp.sum(summed * summed, axis=1)), "tp"
    )
    row_mean = first_sum / D
    row_var = square_sum / D - row_mean * row_mean
    offset = lax.axis_index("tp") * feat_width
    gain_part = lax.dynamic_slice_in_dim(ln_gain, offset, feat_width, 0)
    bias_part = lax.dynamic_slice_in_dim(ln_bias, offset, feat_width, 0)
    scaled = (summed - row_mean[:, None]) / jnp.sqrt(row_var[:, None] + 1e-05)
    return (scaled * gain_part + bias_part).astype(jnp.bfloat16)


def shards(
    tokens, placement, cache_len, w_query, w_key, w_value, w_out, k_cache, v_cache, ln_gain, ln_bias
):
    row_count, feat_width = tokens.shape
    block_count = placement.shape[0]
    block_rows = row_count // block_count
    per_peer = block_count // lax.axis_size("req")
    send_slot = placement // block_count * per_peer + placement % per_peer
    send_order = (
        jnp.zeros((block_count,), jnp.int32)
        .at[send_slot]
        .set(jnp.arange(block_count, dtype=jnp.int32))
    )

    def to_blocks(array):
        return array.reshape(block_count, block_rows, array.shape[1])

    arrived = lax.all_to_all(
        to_blocks(tokens)[send_order], "req", split_axis=0, concat_axis=0, tiled=True
    ).reshape(row_count, feat_width)
    whole = lax.all_gather(arrived, "tp", axis=1, tiled=True)
    queries, new_keys, new_values = project_rows(whole, w_query, w_key, w_value)
    context = attend_all(queries, new_keys, new_values, k_cache, v_cache, cache_len)
    normed = finish_rows(context, arrived, w_out, ln_gain, ln_bias)
    returned = lax.all_to_all(to_blocks(normed), "req", split_axis=0, concat_axis=0, tiled=True)
    return returned[send_slot].reshape(row_count, feat_width)


def solution(mesh):
    in_specs = (
        P("req", "tp"),
        P("req"),
        P("req"),
        P(None, "tp"),
        P(None, "tp"),
        P(None, "tp"),
        P("tp", None),
        P("req", None, "tp"),
        P("req", None, "tp"),
        P(),
        P(),
    )
    out_specs = P("req", "tp")
    return jax.shard_map(shards, mesh=mesh, in_specs=in_specs, out_specs=out_specs, check_vma=False)
```

profile of v0, /device:TPU:2, one launch (start us, length us, event | category | flops | bytes accessed | tf_op | source)
XLA Modules:
  0.0 176.9 jit_solution(9790313830979759242)
XLA Ops:
  7.3 1.0 scatter_custom_fusion
  8.3 1.0 reshape.143
  10.1 32.7 %all_to_all.10 = bf16[128,4,256]{2,1,0:T(4,128)(2,1)S(1)} all-to-all(bf16[128,4,256]{2,1,0:T(4,128)(2,1)S(1)} %gather_fusion), channel_id=1, replica_groups=mesh['req'=128,'tp'=4] {'req'}, dimensions={0} | all-to-all | bytes 524288 | tf_op jit(solution)/shard_map/all_to_all | solution.py:98
  43.7 22.3 %all-gather.2.cloned.1.call-done = bf16[512,1024]{1,0:T(8,128)(2,1)} async-done(((bf16[512,256]{1,0:T(8,128)(2,1)}), bf16[512,1024]{1,0:T(8,128)(2,1)}) %all-gather.2.cloned.1.call-update) | async-done | bytes 1048592 | tf_op jit(solution)/shard_map/all_gather | solution.py:101
  66.0 2.5 %convolution_convert_fusion.2 = bf16[512,256]{1,0:T(8,128)(2,1)} fusion(bf16[512,1024]{1,0:T(8,128)(2,1)} %all-gather.2.cloned.1.call-done, bf16[1024,256]{1,0:T(8,128)(2,1)S(1)} %copy-done.8), kind=kOutput, calls=%fused_computation.43 | convolution fusion | flops 268566528 | bytes 1835008 | tf_op jit(solution)/shard_map/dot_general | solution.py:56
  68.4 1.1 convolution_convert_fusion.1
  69.6 1.1 convolution_convert_fusion.3
  70.8 23.4 %while.12 = (s32[]{:T(128)}, bf16[2,256,256]{2,1,0:T(8,128)(2,1)}, bf16[2,1024,256]{2,1,0:T(8,128)(2,1)S(1)}, bf16[2,256,256]{2,1,0:T(8,128)(2,1)}, s32[2]{0:T(1...) while((s32[]{:T(128)}, bf16[2,256,256]{2,1,0:T(8,128)(2,1)}, ...), condition=%wide.region_4.5_spmd, body=%wide.region_1.4_spmd.sunk | while | flops 521149696 | bytes 12803309 | solution.py:41
  72.4 1.1 constant_dynamic-slice_fusion.9
  73.7 1.0 constant_dynamic-slice_fusion.10
  74.9 2.3 %fusion.77 = f32[4,256]{1,0:T(4,128)S(1)} fusion(pred[256,1280]{1,0:T(8,128)(4,1)S(1)} %fusion.76, bf16[256,4,64]{0,2,1:T(8,128)(2,1)S(1)} %bitcast.53, bf16[256,4,64]{0,2,1:T(8,128)(2,1)S(1)} %bitcast.55, bf16[1024,4,64]{0,2,1:T(8,128)(2,1)S(1)} %bitcast.50), kind=kOutput, calls=%fused_computation.7.clone.1 | convolution fusion | flops 175637760 | bytes 1118208 | tf_op jit(solution)/shard_map/while/body/eval_jaxpr/sub | solution.py:29
  77.5 0.9 constant_dynamic-slice_fusion.8
  78.5 3.1 %fusion.78 = bf16[256,4,64]{0,2,1:T(8,128)(2,1)S(1)} fusion(pred[256,1280]{1,0:T(8,128)(4,1)S(1)} %fusion.76, bf16[256,4,64]{0,2,1:T(8,128)(2,1)S(1)} %bitcast.57, bf16[1024,4,64]{0,2,1:T(8,128)(2,1)S(1)} %bitcast.52, bf16[256,4,64]{0,2,1:T(8,128)(2,1)} %bitcast.54, bf16[256,4,64]{0,2,1:T(8,128)(2,1)} %bitcast.56, ...), kind=kOutput, calls=%fused_computation.16.clone.1 | convolution fusion | flops 344852736 | bytes 1904640 | tf_op jit(solution)/shard_map/while/body/eval_jaxpr/hqk,khd->qhd/dot_general | solution.py:31
  84.1 1.1 constant_dynamic-slice_fusion.9
  85.4 1.0 constant_dynamic-slice_fusion.10
  86.7 2.3 %fusion.77 = f32[4,256]{1,0:T(4,128)S(1)} fusion(pred[256,1280]{1,0:T(8,128)(4,1)S(1)} %fusion.76, bf16[256,4,64]{0,2,1:T(8,128)(2,1)S(1)} %bitcast.53, bf16[256,4,64]{0,2,1:T(8,128)(2,1)S(1)} %bitcast.55, bf16[1024,4,64]{0,2,1:T(8,128)(2,1)S(1)} %bitcast.50), kind=kOutput, calls=%fused_computation.7.clone.1 | convolution fusion | flops 175637760 | bytes 1118208 | tf_op jit(solution)/shard_map/while/body/eval_jaxpr/sub | solution.py:29
  90.3 3.1 %fusion.78 = bf16[256,4,64]{0,2,1:T(8,128)(2,1)S(1)} fusion(pred[256,1280]{1,0:T(8,128)(4,1)S(1)} %fusion.76, bf16[256,4,64]{0,2,1:T(8,128)(2,1)S(1)} %bitcast.57, bf16[1024,4,64]{0,2,1:T(8,128)(2,1)S(1)} %bitcast.52, bf16[256,4,64]{0,2,1:T(8,128)(2,1)} %bitcast.54, bf16[256,4,64]{0,2,1:T(8,128)(2,1)} %bitcast.56, ...), kind=kOutput, calls=%fused_computation.16.clone.1 | convolution fusion | flops 344852736 | bytes 1904640 | tf_op jit(solution)/shard_map/while/body/eval_jaxpr/hqk,khd->qhd/dot_general | solution.py:31
  94.2 2.4 %convolution_convert_fusion = bf16[512,1024]{1,0:T(8,128)(2,1)} fusion(bf16[512,256]{1,0:T(8,128)(2,1)} %bitcast.62, bf16[256,1024]{1,0:T(8,128)(2,1)S(1)} %copy-done), kind=kOutput, calls=%fused_computation.41 | convolution fusion | flops 268959744 | bytes 1835008 | tf_op jit(solution)/shard_map/dot_general | solution.py:64
  98.2 27.0 %reduce-scatter.2.cloned.1.call-done = bf16[512,256]{1,0:T(8,128)(2,1)} async-done(((bf16[512,1024]{1,0:T(8,128)(2,1)}), bf16[512,256]{1,0:T(8,128)(2,1)}) %reduce-scatter.2.cloned.1.call-update) | async-done | bytes 262160 | tf_op jit(solution)/shard_map/reduce_scatter | solution.py:65
  125.2 1.2 fusion.46
  126.4 10.6 %all-reduce = (f32[512]{0:T(512)S(1)}, f32[512]{0:T(512)S(1)}) all-reduce(f32[512]{0:T(512)S(1)} %get-tuple-element.124, f32[512]{0:T(512)S(1)} %get-tuple-element.123), channel_id=1, replica_groups=mesh['req'=128,'tp'=4] {'tp'}, use_global_device_ids=true, to_apply=%region_9.10 | all-reduce | flops 1024 | bytes 8192 | tf_op jit(solution)/shard_map/psum | solution.py:69
  137.0 1.2 add_convert_fusion
  138.9 14.5 %all-to-all-start.1 = ((bf16[128,4,256]{2,1,0:T(4,128)(2,1)}), bf16[128,4,256]{2,1,0:T(4,128)(2,1)S(1)}, u32[]{:S(2)}, u32[]{:S(2)}) async-start(bf16[128,4,256]{2,1,0:T(4,128)(2,1)} %reshape.149), calls=%async_computation.2 | async-start | bytes 524288 | tf_op jit(solution)/shard_map/all_to_all | solution.py:105
  153.4 15.1 %all-to-all-done.1 = bf16[128,4,256]{2,1,0:T(4,128)(2,1)S(1)} async-done(((bf16[128,4,256]{2,1,0:T(4,128)(2,1)}), bf16[128,4,256]{2,1,0:T(4,128)(2,1)S(1)}, u32[]{:S(2)}, u32[]{:S(2)}) %all-to-all-start.1) | async-done | bytes 262176 | tf_op jit(solution)/shard_map/all_to_all | solution.py:105
  (73 shorter events, 13.5 us)
Async XLA Ops:
  6.5 87.7 %copy-start = (bf16[256,1024]{1,0:T(8,128)(2,1)S(1)}, bf16[256,1024]{1,0:T(8,128)(2,1)}, u32[]{:S(2)}) copy-start(bf16[256,1024]{1,0:T(8,128)(2,1)} %param.19) | copy-start | bytes 1572868
  6.5 59.4 %all-gather.2.cloned.1.call-start = ((), (), s32[]{:S(2)}) async-start(), calls=%async_computation.3 | async-start | bytes 1310720 | tf_op jit(solution)/shard_map/all_gather | solution.py:101
  9.3 56.7 %copy-start.8 = (bf16[1024,256]{1,0:T(8,128)(2,1)S(1)}, bf16[1024,256]{1,0:T(8,128)(2,1)}, u32[]{:S(2)}) copy-start(bf16[1024,256]{1,0:T(8,128)(2,1)} %param.16) | copy-start | bytes 1572868
  43.6 24.8 %copy-start.9 = (bf16[1024,256]{1,0:T(8,128)(2,1)S(1)}, bf16[1024,256]{1,0:T(8,128)(2,1)}, u32[]{:S(2)}) copy-start(bf16[1024,256]{1,0:T(8,128)(2,1)} %param.17) | copy-start | bytes 1572868
  43.6 81.6 %reduce-scatter.2.cloned.1.call-start = ((), (), s32[]{:S(2)}) async-start(), calls=%async_computation.4 | async-start | bytes 1310720 | tf_op jit(solution)/shard_map/reduce_scatter | solution.py:65
  65.9 2.5 %copy-start.7 = (bf16[512,1024]{1,0:T(8,128)(2,1)S(1)}, bf16[512,1024]{1,0:T(8,128)(2,1)}, u32[]{:S(2)}) copy-start(bf16[512,1024]{1,0:T(8,128)(2,1)} %all-gather.2.cloned.1.call-done) | copy-start | bytes 3145732
  68.4 1.1 copy-start.10
  69.6 1.2 copy-start.1
  69.6 1.2 copy-start.11
  74.8 2.5 %copy-start.3 = (bf16[1,256,256]{1,2,0:T(8,128)(2,1)}, bf16[1,256,256]{1,2,0:T(8,128)(2,1)S(1)}, u32[]{:S(2)}) copy-start(bf16[1,256,256]{1,2,0:T(8,128)(2,1)S(1)} %copy.38) | copy-start | bytes 393220 | tf_op jit(solution)/shard_map/while
  74.9 2.3 %copy-start.4 = (bf16[1,256,256]{1,2,0:T(8,128)(2,1)}, bf16[1,256,256]{1,2,0:T(8,128)(2,1)S(1)}, u32[]{:S(2)}) copy-start(bf16[1,256,256]{1,2,0:T(8,128)(2,1)S(1)} %copy.39) | copy-start | bytes 393220 | tf_op jit(solution)/shard_map/while
  78.5 3.3 %copy-start.5 = (bf16[2,256,256]{2,1,0:T(8,128)(2,1)S(1)}, bf16[2,256,256]{2,1,0:T(8,128)(2,1)}, u32[]{:S(2)}) copy-start(bf16[2,256,256]{2,1,0:T(8,128)(2,1)} %get-tuple-element.222) | copy-start | bytes 786436 | tf_op jit(solution)/shard_map/while
  81.8 0.7 copy-start.6
  86.5 2.5 %copy-start.3 = (bf16[1,256,256]{1,2,0:T(8,128)(2,1)}, bf16[1,256,256]{1,2,0:T(8,128)(2,1)S(1)}, u32[]{:S(2)}) copy-start(bf16[1,256,256]{1,2,0:T(8,128)(2,1)S(1)} %copy.38) | copy-start | bytes 393220 | tf_op jit(solution)/shard_map/while
  86.6 2.3 %copy-start.4 = (bf16[1,256,256]{1,2,0:T(8,128)(2,1)}, bf16[1,256,256]{1,2,0:T(8,128)(2,1)S(1)}, u32[]{:S(2)}) copy-start(bf16[1,256,256]{1,2,0:T(8,128)(2,1)S(1)} %copy.39) | copy-start | bytes 393220 | tf_op jit(solution)/shard_map/while
  90.2 3.3 %copy-start.5 = (bf16[2,256,256]{2,1,0:T(8,128)(2,1)S(1)}, bf16[2,256,256]{2,1,0:T(8,128)(2,1)}, u32[]{:S(2)}) copy-start(bf16[2,256,256]{2,1,0:T(8,128)(2,1)} %get-tuple-element.222) | copy-start | bytes 786436 | tf_op jit(solution)/shard_map/while
  93.5 0.7 copy-start.6
  94.2 31.0 %copy-start.2 = (bf16[512,256]{1,0:T(8,128)(2,1)S(1)}, bf16[512,256]{1,0:T(8,128)(2,1)}, u32[]{:S(2)}) copy-start(bf16[512,256]{1,0:T(8,128)(2,1)} %reshape.144) | copy-start | bytes 786436
  138.9 29.6 %all-to-all-start.1 = ((bf16[128,4,256]{2,1,0:T(4,128)(2,1)}), bf16[128,4,256]{2,1,0:T(4,128)(2,1)S(1)}, u32[]{:S(2)}, u32[]{:S(2)}) async-start(bf16[128,4,256]{2,1,0:T(4,128)(2,1)} %reshape.149), calls=%async_computation.2 | async-start | bytes 524288 | tf_op jit(solution)/shard_map/all_to_all | solution.py:105
Sparse Core Ops, SparseCore 0:
  43.7 22.1 all-gather.1
  96.8 28.3 reduce-scatter.1
where the time goes:
time: 178 us; the launch traced here: 177 us
  waiting for transfers between devices  64.4 us (36%)
  blocking collectives  43.3 us (24%)
  matrix products  18.1 us (10%)
  local copies, waits for them, and re-layouts  18 us (10%)
  starting transfers between devices  14.5 us (8%)
  between operations  13.5 us (8%)
  other arithmetic  4.9 us (3%)
    all_to_all x1, blocking collectives, shards(): lax.all_to_all(to_blocks(tokens)[send_order], 'req', split_axis=0, concat...  32.7 us
    reduce_scatter x1, waiting for transfers between devices, finish_rows(): lax.psum_scatter(partial_sum.astype(jnp.bfloat16), 'tp', scatter_dimensio...  27 us
    all_gather x1, waiting for transfers between devices, shards(): whole = lax.all_gather(arrived, 'tp', axis=1, tiled=True)  22.3 us
    all_to_all x1, waiting for transfers between devices, shards(): lax.all_to_all(to_blocks(normed), 'req', split_axis=0, concat_axis=0, til...  15.1 us
    all_to_all x1, starting transfers between devices, shards(): lax.all_to_all(to_blocks(normed), 'req', split_axis=0, concat_axis=0, til...  14.5 us
    psum x1, blocking collectives, finish_rows(): lax.psum((jnp.sum(summed, axis=1), jnp.sum(summed * summed, axis=1)), 'tp')  10.6 us
    dynamic_slice x18, local copies, waits for them, and re-layouts, attend_all(): lax.map(lambda items: attend_padded(*items), (queries.reshape(req_shape),...  8.77 us
    dot_general x2, matrix products, attend_padded(): jnp.einsum('hqk,khd->qhd', weight.astype(jnp.bfloat16), values_all, prefe...  6.26 us
  transfers between devices with their start and end apart: 3, of which 3 were waited for; matrix products, arithmetic and copies ran while one was open for 1% of the time, Pallas kernels for 0%

commit v1 on v0

--- a/solution.py
+++ b/solution.py
@@ -5,6 +5,28 @@
 
 D = 1024
 HEADS = 16
+
+
+def in_order(blocks, dim):
+    shape = list(blocks.shape[1:])
+    shape[dim] *= blocks.shape[0]
+    return jnp.moveaxis(blocks, 0, dim).reshape(shape)
+
+
+def gather_around(shard, axis, dim):
+    size = lax.axis_size(axis)
+    pairs = [(i, (i + 1) % size) for i in range(size)]
+    back = [(b, a) for a, b in pairs]
+    lower, upper = ([], [])
+    for hop in range(size - 1):
+        if hop % 2 == 0:
+            lower.append(lax.ppermute(lower[-1] if lower else shard, axis, pairs))
+        else:
+            upper.append(lax.ppermute(upper[-1] if upper else shard, axis, back))
+    tiles = jnp.stack([*lower[::-1], shard, *upper])
+    shift = lax.axis_index(axis) - len(lower)
+    tiles = tiles[(jnp.arange(size) - shift) % size]
+    return in_order(tiles, dim)
 
 
 def head_view(array, head_size):
@@ -98,7 +120,7 @@
     arrived = lax.all_to_all(
         to_blocks(tokens)[send_order], "req", split_axis=0, concat_axis=0, tiled=True
     ).reshape(row_count, feat_width)
-    whole = lax.all_gather(arrived, "tp", axis=1, tiled=True)
+    whole = gather_around(arrived, "tp", 1)
     queries, new_keys, new_values = project_rows(whole, w_query, w_key, w_value)
     context = attend_all(queries, new_keys, new_values, k_cache, v_cache, cache_len)
     normed = finish_rows(context, arrived, w_out, ln_gain, ln_bias)

time: 178 us -> 165 us (0.927)
  waiting for transfers between devices: 64.4 us -> 42.6 us
  starting transfers between devices: 14.5 us -> 23.8 us
    all_gather x1 -> x0, waiting for transfers between devices: 22.3 us -> none  [shards(): whole = lax.all_gather(arrived, 'tp', axis=1, tiled=True)]
    ppermute x0 -> x3, starting transfers between devices: none -> 9.23 us  [the longest x2 6.79 us: gather_around(): lower.append(lax.ppermute(lower[-1] if lower else shard, axis, pairs))]
    ppermute x0 -> x3, waiting for transfers between devices: none -> 7.82 us  [the longest x2 7.82 us: gather_around(): lower.append(lax.ppermute(lower[-1] if lower else shard, axis, pairs))]
    reduce_scatter x1, waiting for transfers between devices: 27 us -> 19.7 us  [finish_rows(): lax.psum_scatter(partial_sum.astype(jnp.bfloat16), 'tp', scatter_dimensio...]
  transfers between devices with their start and end apart: 3 -> 5, of which waited for: 3 -> 4; matrix products, arithmetic and copies ran while one was open for 1% -> 1% of each run, Pallas kernels for 0% -> 0%
where the time goes in v1:
time: 165 us; the launch traced here: 164 us
  blocking collectives  43.3 us (26%)
  waiting for transfers between devices  42.6 us (26%)
  starting transfers between devices  23.8 us (14%)
  local copies, waits for them, and re-layouts  19 us (12%)
  matrix products  16.9 us (10%)
  between operations  13.6 us (8%)
  other arithmetic  4.95 us (3%)
    all_to_all x1, blocking collectives, shards(): lax.all_to_all(to_blocks(tokens)[send_order], 'req', split_axis=0, concat...  32.7 us
    reduce_scatter x1, waiting for transfers between devices, finish_rows(): lax.psum_scatter(partial_sum.astype(jnp.bfloat16), 'tp', scatter_dimensio...  19.7 us
    all_to_all x1, waiting for transfers between devices, shards(): lax.all_to_all(to_blocks(normed), 'req', split_axis=0, concat_axis=0, til...  15.1 us
    all_to_all x1, starting transfers between devices, shards(): lax.all_to_all(to_blocks(normed), 'req', split_axis=0, concat_axis=0, til...  14.6 us
    psum x1, blocking collectives, finish_rows(): lax.psum((jnp.sum(summed, axis=1), jnp.sum(summed * summed, axis=1)), 'tp')  10.6 us
    dynamic_slice x18, local copies, waits for them, and re-layouts, attend_all(): lax.map(lambda items: attend_padded(*items), (queries.reshape(req_shape),...  8.75 us
    ppermute x2, waiting for transfers between devices, gather_around(): lower.append(lax.ppermute(lower[-1] if lower else shard, axis, pairs))  7.82 us
    ppermute x2, starting transfers between devices, gather_around(): lower.append(lax.ppermute(lower[-1] if lower else shard, axis, pairs))  6.79 us
  transfers between devices with their start and end apart: 5, of which 4 were waited for; matrix products, arithmetic and copies ran while one was open for 1% of the time, Pallas kernels for 0%

profile of v1, /device:TPU:2, one launch (start us, length us, event | category | flops | bytes accessed | tf_op | source)
XLA Modules:
  0.0 164.3 jit_solution(2547496268408411676)
XLA Ops:
  8.3 1.0 reshape.195
  10.1 32.7 %all_to_all.10 = bf16[128,4,256]{2,1,0:T(4,128)(2,1)S(1)} all-to-all(bf16[128,4,256]{2,1,0:T(4,128)(2,1)S(1)} %gather_fusion), channel_id=1, replica_groups=mesh['req'=128,'tp'=4] {'req'}, dimensions={0} | all-to-all | bytes 524288 | tf_op jit(solution)/shard_map/all_to_all | solution.py:120
  42.9 3.4 %collective-permute-start = (bf16[512,256]{1,0:T(8,128)(2,1)S(1)}, bf16[512,256]{1,0:T(8,128)(2,1)S(1)}, u32[]{:S(2)}, u32[]{:S(2)}) collective-permute-start(bf16[512,256]{1,0:T(8,128)(2,1)S(1)} %reshape.196), channel_id=1, source_target_pairs={{0,1},{1,2},{2,3},{3,0},{4,5},{5,6},{6,7},{7,4},{8,9},{9,10},{10,1... | collective-permute-start | bytes 786440 | tf_op jit(solution)/shard_map/ppermute | solution.py:23
  46.3 2.4 %collective-permute-start.2 = (bf16[512,256]{1,0:T(8,128)(2,1)S(1)}, bf16[512,256]{1,0:T(8,128)(2,1)S(1)}, u32[]{:S(2)}, u32[]{:S(2)}) collective-permute-start(bf16[512,256]{1,0:T(8,128)(2,1)S(1)} %reshape.196), channel_id=1, source_target_pairs={{1,0},{2,1},{3,2},{0,3},{5,4},{6,5},{7,6},{4,7},{9,8},{10,9},{11,1... | collective-permute-start | bytes 786440 | tf_op jit(solution)/shard_map/ppermute | solution.py:25
  48.8 3.1 %collective-permute-done = bf16[512,256]{1,0:T(8,128)(2,1)S(1)} collective-permute-done((bf16[512,256]{1,0:T(8,128)(2,1)S(1)}, bf16[512,256]{1,0:T(8,128)(2,1)S(1)}, u32[]{:S(2)}, u32[]{:S(2)}) %collective-permute-start) | collective-permute-done | bytes 262176 | tf_op jit(solution)/shard_map/ppermute | solution.py:23
  51.9 3.4 %collective-permute-start.1 = (bf16[512,256]{1,0:T(8,128)(2,1)S(1)}, bf16[512,256]{1,0:T(8,128)(2,1)S(1)}, u32[]{:S(2)}, u32[]{:S(2)}) collective-permute-start(bf16[512,256]{1,0:T(8,128)(2,1)S(1)} %collective-permute-done), channel_id=1, source_target_pairs={{0,1},{1,2},{2,3},{3,0},{4,5},{5,6},{6,7},{7,4},{8,9},{9,10},{10,1... | collective-permute-start | bytes 786440 | tf_op jit(solution)/shard_map/ppermute | solution.py:23
  55.4 4.7 %collective-permute-done.1 = bf16[512,256]{1,0:T(8,128)(2,1)S(1)} collective-permute-done((bf16[512,256]{1,0:T(8,128)(2,1)S(1)}, bf16[512,256]{1,0:T(8,128)(2,1)S(1)}, u32[]{:S(2)}, u32[]{:S(2)}) %collective-permute-start.1) | collective-permute-done | bytes 262176 | tf_op jit(solution)/shard_map/ppermute | solution.py:23
  61.9 1.2 convolution_convert_fusion.3
  63.1 1.2 convolution_convert_fusion.2
  64.3 1.2 convolution_convert_fusion.1
  65.5 23.3 %while.12 = (s32[]{:T(128)}, bf16[2,256,256]{2,1,0:T(8,128)(2,1)}, bf16[2,1024,256]{2,1,0:T(8,128)(2,1)S(1)}, bf16[2,256,256]{2,1,0:T(8,128)(2,1)}, s32[2]{0:T(1...) while((s32[]{:T(128)}, bf16[2,256,256]{2,1,0:T(8,128)(2,1)}, ...), condition=%wide.region_4.5_spmd, body=%wide.region_1.4_spmd.sunk | while | flops 521149696 | bytes 12803309 | solution.py:63
  67.0 1.1 constant_dynamic-slice_fusion.9
  69.6 2.3 %fusion.79 = f32[4,256]{1,0:T(4,128)S(1)} fusion(pred[256,1280]{1,0:T(8,128)(4,1)S(1)} %fusion.78, bf16[256,4,64]{0,2,1:T(8,128)(2,1)S(1)} %bitcast.61, bf16[256,4,64]{0,2,1:T(8,128)(2,1)S(1)} %bitcast.63, bf16[1024,4,64]{0,2,1:T(8,128)(2,1)S(1)} %bitcast.57), kind=kOutput, calls=%fused_computation.8.clone.1 | convolution fusion | flops 175637760 | bytes 1118208 | tf_op jit(solution)/shard_map/while/body/eval_jaxpr/sub | solution.py:51
  73.2 3.1 %fusion.80 = bf16[256,4,64]{0,2,1:T(8,128)(2,1)S(1)} fusion(pred[256,1280]{1,0:T(8,128)(4,1)S(1)} %fusion.78, bf16[256,4,64]{0,2,1:T(8,128)(2,1)S(1)} %bitcast.65, bf16[1024,4,64]{0,2,1:T(8,128)(2,1)S(1)} %bitcast.59, bf16[256,4,64]{0,2,1:T(8,128)(2,1)} %bitcast.62, bf16[256,4,64]{0,2,1:T(8,128)(2,1)} %bitcast.64, ...), kind=kOutput, calls=%fused_computation.17.clone.1 | convolution fusion | flops 344852736 | bytes 1904640 | tf_op jit(solution)/shard_map/while/body/eval_jaxpr/hqk,khd->qhd/dot_general | solution.py:53
  78.7 1.1 constant_dynamic-slice_fusion.9
  81.2 2.3 %fusion.79 = f32[4,256]{1,0:T(4,128)S(1)} fusion(pred[256,1280]{1,0:T(8,128)(4,1)S(1)} %fusion.78, bf16[256,4,64]{0,2,1:T(8,128)(2,1)S(1)} %bitcast.61, bf16[256,4,64]{0,2,1:T(8,128)(2,1)S(1)} %bitcast.63, bf16[1024,4,64]{0,2,1:T(8,128)(2,1)S(1)} %bitcast.57), kind=kOutput, calls=%fused_computation.8.clone.1 | convolution fusion | flops 175637760 | bytes 1118208 | tf_op jit(solution)/shard_map/while/body/eval_jaxpr/sub | solution.py:51
  84.8 3.1 %fusion.80 = bf16[256,4,64]{0,2,1:T(8,128)(2,1)S(1)} fusion(pred[256,1280]{1,0:T(8,128)(4,1)S(1)} %fusion.78, bf16[256,4,64]{0,2,1:T(8,128)(2,1)S(1)} %bitcast.65, bf16[1024,4,64]{0,2,1:T(8,128)(2,1)S(1)} %bitcast.59, bf16[256,4,64]{0,2,1:T(8,128)(2,1)} %bitcast.62, bf16[256,4,64]{0,2,1:T(8,128)(2,1)} %bitcast.64, ...), kind=kOutput, calls=%fused_computation.17.clone.1 | convolution fusion | flops 344852736 | bytes 1904640 | tf_op jit(solution)/shard_map/while/body/eval_jaxpr/hqk,khd->qhd/dot_general | solution.py:53
  88.8 2.4 %convolution_convert_fusion = bf16[512,1024]{1,0:T(8,128)(2,1)} fusion(bf16[512,256]{1,0:T(8,128)(2,1)} %bitcast.73, bf16[256,1024]{1,0:T(8,128)(2,1)S(1)} %copy-done), kind=kOutput, calls=%fused_computation.42 | convolution fusion | flops 268959744 | bytes 1835008 | tf_op jit(solution)/shard_map/dot_general | solution.py:86
  92.8 19.7 %reduce-scatter.2.cloned.1.call-done = bf16[512,256]{1,0:T(8,128)(2,1)} async-done(((bf16[512,1024]{1,0:T(8,128)(2,1)}), bf16[512,256]{1,0:T(8,128)(2,1)}) %reduce-scatter.2.cloned.1.call-update) | async-done | bytes 262160 | tf_op jit(solution)/shard_map/reduce_scatter | solution.py:87
  112.5 1.2 fusion.46
  113.6 10.6 %all-reduce = (f32[512]{0:T(512)S(1)}, f32[512]{0:T(512)S(1)}) all-reduce(f32[512]{0:T(512)S(1)} %get-tuple-element.124, f32[512]{0:T(512)S(1)} %get-tuple-element.123), channel_id=1, replica_groups=mesh['req'=128,'tp'=4] {'tp'}, use_global_device_ids=true, to_apply=%region_9.10 | all-reduce | flops 1024 | bytes 8192 | tf_op jit(solution)/shard_map/psum | solution.py:91
  124.2 1.2 add_convert_fusion
  126.2 14.6 %all-to-all-start.1 = ((bf16[128,4,256]{2,1,0:T(4,128)(2,1)}), bf16[128,4,256]{2,1,0:T(4,128)(2,1)S(1)}, u32[]{:S(2)}, u32[]{:S(2)}) async-start(bf16[128,4,256]{2,1,0:T(4,128)(2,1)} %reshape.202), calls=%async_computation.2 | async-start | bytes 524288 | tf_op jit(solution)/shard_map/all_to_all | solution.py:127
  140.7 15.1 %all-to-all-done.1 = bf16[128,4,256]{2,1,0:T(4,128)(2,1)S(1)} async-done(((bf16[128,4,256]{2,1,0:T(4,128)(2,1)}), bf16[128,4,256]{2,1,0:T(4,128)(2,1)S(1)}, u32[]{:S(2)}, u32[]{:S(2)}) %all-to-all-start.1) | async-done | bytes 262176 | tf_op jit(solution)/shard_map/all_to_all | solution.py:127
  (82 shorter events, 18.4 us)
Async XLA Ops:
  6.5 82.3 %copy-start = (bf16[256,1024]{1,0:T(8,128)(2,1)S(1)}, bf16[256,1024]{1,0:T(8,128)(2,1)}, u32[]{:S(2)}) copy-start(bf16[256,1024]{1,0:T(8,128)(2,1)} %param.19) | copy-start | bytes 1572868
  6.5 105.9 %reduce-scatter.2.cloned.1.call-start = ((), (), s32[]{:S(2)}) async-start(), calls=%async_computation.3 | async-start | bytes 1310720 | tf_op jit(solution)/shard_map/reduce_scatter | solution.py:87
  42.9 17.2 %copy-start.4 = (bf16[512,256]{1,0:T(8,128)(2,1)}, bf16[512,256]{1,0:T(8,128)(2,1)S(1)}, u32[]{:S(2)}) copy-start(bf16[512,256]{1,0:T(8,128)(2,1)S(1)} %reshape.196) | copy-start | bytes 786436
  42.9 8.9 %collective-permute-start = (bf16[512,256]{1,0:T(8,128)(2,1)S(1)}, bf16[512,256]{1,0:T(8,128)(2,1)S(1)}, u32[]{:S(2)}, u32[]{:S(2)}) collective-permute-start(bf16[512,256]{1,0:T(8,128)(2,1)S(1)} %reshape.196), channel_id=1, source_target_pairs={{0,1},{1,2},{2,3},{3,0},{4,5},{5,6},{6,7},{7,4},{8,9},{9,10},{10,1... | collective-permute-start | bytes 786440 | tf_op jit(solution)/shard_map/ppermute | solution.py:23
  46.3 9.1 %collective-permute-start.2 = (bf16[512,256]{1,0:T(8,128)(2,1)S(1)}, bf16[512,256]{1,0:T(8,128)(2,1)S(1)}, u32[]{:S(2)}, u32[]{:S(2)}) collective-permute-start(bf16[512,256]{1,0:T(8,128)(2,1)S(1)} %reshape.196), channel_id=1, source_target_pairs={{1,0},{2,1},{3,2},{0,3},{5,4},{6,5},{7,6},{4,7},{9,8},{10,9},{11,1... | collective-permute-start | bytes 786440 | tf_op jit(solution)/shard_map/ppermute | solution.py:25
  51.9 8.3 %collective-permute-start.1 = (bf16[512,256]{1,0:T(8,128)(2,1)S(1)}, bf16[512,256]{1,0:T(8,128)(2,1)S(1)}, u32[]{:S(2)}, u32[]{:S(2)}) collective-permute-start(bf16[512,256]{1,0:T(8,128)(2,1)S(1)} %collective-permute-done), channel_id=1, source_target_pairs={{0,1},{1,2},{2,3},{3,0},{4,5},{5,6},{6,7},{7,4},{8,9},{9,10},{10,1... | collective-permute-start | bytes 786440 | tf_op jit(solution)/shard_map/ppermute | solution.py:23
  60.9 1.0 copy-start.8
  61.9 1.2 copy-start.9
  63.1 1.2 copy-start.10
  64.3 1.2 copy-start.1
  64.3 1.2 copy-start.11
  69.5 2.5 %copy-start.2 = (bf16[1,256,256]{1,2,0:T(8,128)(2,1)}, bf16[1,256,256]{1,2,0:T(8,128)(2,1)S(1)}, u32[]{:S(2)}) copy-start(bf16[1,256,256]{1,2,0:T(8,128)(2,1)S(1)} %copy.39) | copy-start | bytes 393220 | tf_op jit(solution)/shard_map/while
  69.6 2.3 %copy-start.3 = (bf16[1,256,256]{1,2,0:T(8,128)(2,1)}, bf16[1,256,256]{1,2,0:T(8,128)(2,1)S(1)}, u32[]{:S(2)}) copy-start(bf16[1,256,256]{1,2,0:T(8,128)(2,1)S(1)} %copy.40) | copy-start | bytes 393220 | tf_op jit(solution)/shard_map/while
  73.2 3.3 %copy-start.6 = (bf16[2,256,256]{2,1,0:T(8,128)(2,1)S(1)}, bf16[2,256,256]{2,1,0:T(8,128)(2,1)}, u32[]{:S(2)}) copy-start(bf16[2,256,256]{2,1,0:T(8,128)(2,1)} %get-tuple-element.222) | copy-start | bytes 786436 | tf_op jit(solution)/shard_map/while
  76.5 0.7 copy-start.7
  81.1 2.5 %copy-start.2 = (bf16[1,256,256]{1,2,0:T(8,128)(2,1)}, bf16[1,256,256]{1,2,0:T(8,128)(2,1)S(1)}, u32[]{:S(2)}) copy-start(bf16[1,256,256]{1,2,0:T(8,128)(2,1)S(1)} %copy.39) | copy-start | bytes 393220 | tf_op jit(solution)/shard_map/while
  81.2 2.3 %copy-start.3 = (bf16[1,256,256]{1,2,0:T(8,128)(2,1)}, bf16[1,256,256]{1,2,0:T(8,128)(2,1)S(1)}, u32[]{:S(2)}) copy-start(bf16[1,256,256]{1,2,0:T(8,128)(2,1)S(1)} %copy.40) | copy-start | bytes 393220 | tf_op jit(solution)/shard_map/while
  84.8 3.3 %copy-start.6 = (bf16[2,256,256]{2,1,0:T(8,128)(2,1)S(1)}, bf16[2,256,256]{2,1,0:T(8,128)(2,1)}, u32[]{:S(2)}) copy-start(bf16[2,256,256]{2,1,0:T(8,128)(2,1)} %get-tuple-element.222) | copy-start | bytes 786436 | tf_op jit(solution)/shard_map/while
  88.1 0.7 copy-start.7
  88.8 23.6 %copy-start.5 = (bf16[512,256]{1,0:T(8,128)(2,1)S(1)}, bf16[512,256]{1,0:T(8,128)(2,1)}, u32[]{:S(2)}) copy-start(bf16[512,256]{1,0:T(8,128)(2,1)} %copy-done.4) | copy-start | bytes 786436
  126.2 29.7 %all-to-all-start.1 = ((bf16[128,4,256]{2,1,0:T(4,128)(2,1)}), bf16[128,4,256]{2,1,0:T(4,128)(2,1)S(1)}, u32[]{:S(2)}, u32[]{:S(2)}) async-start(bf16[128,4,256]{2,1,0:T(4,128)(2,1)} %reshape.202), calls=%async_computation.2 | async-start | bytes 524288 | tf_op jit(solution)/shard_map/all_to_all | solution.py:127
Sparse Core Ops, SparseCore 0:
  91.4 21.0 reduce-scatter.1
